TPU v7x, 32 devices: a whole 2x2x4 slice. The times are simulated.
32 devices in a mesh: groups: 1, gx: 32 (over z, y, x, core).
Axes of the slice: x: 2, y: 2, z: 4, core: 2. Of those that a mesh axis runs over, the one named last changes fastest.
Arguments:
- solid_state: float32 [9, 2, 1, 256, 4, 128], P(None, None, 'groups', 'gx'), may hold values from -6 to 6
- water_state: float32 [4, 2, 1, 128, 12, 256], P(None, None, 'groups', 'gx'), may hold values from -6 to 6
- lame_lambda: float32 [256, 4, 128], P('gx'), may hold values from 0.4 to 1.2
- shear_mu: float32 [256, 4, 128], P('gx'), may hold values from 0.1 to 0.5
- solid_buoy: float32 [256, 4, 128], P('gx'), may hold values from 0.4 to 1
- water_kappa: float32 [128, 12, 256], P('gx'), may hold values from 0.5 to 1
- water_buoy: float32 [128, 12, 256], P('gx'), may hold values from 0.6 to 1.2
- seafloor: int32 [128, 256], P('gx'), may hold values from 6 to 12
- source_cell: int32 [1], P('groups'), may hold values from 0 to 196607
- wavelet: float32 [4, 1], P(None, 'groups'), may hold values from -48 to 48
- receiver_column: int32 [128], replicated, may hold values from 0 to 32767
- observed: float32 [4, 1, 128], P(None, 'groups'), may hold values from -6 to 6
Outputs:
- grad_lambda: float32 [256, 4, 128], P('gx', 'groups')
- grad_mu: float32 [256, 4, 128], P('gx', 'groups')
- grad_kappa: float32 [128, 12, 256], P('gx', 'groups')
- residuals: float32 [4, 1, 128], P(None, 'groups')
Inputs may be any that keep to these rules, and one draw needn't show every extreme that they name: Every column holds water from z = 0 to z = seafloor - 1 and rock below it. source_cell is (z * 128 + y) * 256 + x of a water cell with z below 6. receiver_column is y * 256 + x; two nodes may share a column.
All inputs are finite; a program needn't handle non-finite values.
Results may differ from a plain program's by a relative error of at most 0.00014.
Values sent between devices are 32-bit elements; how exact they have to be, the bound alone decides.
No kernel may reach another device: no remote copies, remote signals or barrier semaphores. Data moves between devices by JAX's collectives and lax.ppermute only.
A program may use at most 64 MiB of HBM per device.

v0:
```python
import jax
import jax.numpy as jnp
from jax import lax
from jax.sharding import PartitionSpec as P

COEFF = (1225.0 / 1024.0, -245.0 / 3072.0, 49.0 / 5120.0, -5.0 / 7168.0)
TIME_STEP = 0.2


def with_halo(array, sides, width):
    for axis, dim in sides:
        devices, length = (lax.axis_size(axis), array.shape[dim])
        up = [(i, (i + 1) % devices) for i in range(devices - 1)]
        down = [(j, i) for i, j in up]
        last = lax.slice_in_dim(array, length - width, length, axis=dim)
        first = lax.slice_in_dim(array, 0, width, axis=dim)
        before = lax.ppermute(last, axis, up)
        after = lax.ppermute(first, axis, down)
        array = jnp.concatenate([before, array, after], axis=dim)
    return array


def stencil(padded, axis, forward):
    length = padded.shape[axis] - 8
    summed = None
    for offset in range(1, 5):
        if forward:
            front_at, back_at = (4 + offset, 5 - offset)
        else:
            front_at, back_at = (3 + offset, 4 - offset)
        front = lax.slice_in_dim(padded, front_at, front_at + length, axis=axis)
        back = lax.slice_in_dim(padded, back_at, back_at + length, axis=axis)
        addend = COEFF[offset - 1] * (front - back)
        summed = addend if summed is None else summed + addend
    return summed


def padded_zero(field, axis):
    widths = [(0, 0)] * field.ndim
    widths[axis] = (4, 4)
    return jnp.pad(field, widths)


def derive(field, axis, forward):
    return stencil(padded_zero(field, axis), axis, forward)


def on_device(
    solid_state,
    water_state,
    lame_lambda,
    shear_mu,
    solid_buoy,
    water_kappa,
    water_buoy,
    seafloor,
    source_cell,
    wavelet,
    receiver_column,
    observed,
):
    parts = lax.axis_size("gx")
    place = lax.axis_index("gx")
    width_x = solid_state.shape[3]
    total_y = solid_state.shape[5]
    total_x = width_x * parts
    shots = solid_state.shape[2]
    shard_axis = 2
    anchor_y = place * water_state.shape[3]
    anchor_x = 0

    def water_halo(field):
        return with_halo(field, (("gx", 2),), 4)

    def water_derive(field, axis, forward):
        if axis == shard_axis:
            return stencil(water_halo(field), axis, forward)
        return derive(field, axis, forward)

    def solid_halo(stacked):
        return with_halo(stacked, (("gx", 3),), 4)

    vel_x, vel_y, vel_z = (solid_state[0], solid_state[1], solid_state[2])
    sig_xx, sig_yy, sig_zz = (solid_state[3], solid_state[4], solid_state[5])
    sig_xy, sig_xz, sig_yz = (solid_state[6], solid_state[7], solid_state[8])
    pressure, flow_x, flow_y, flow_z = (
        water_state[0],
        water_state[1],
        water_state[2],
        water_state[3],
    )
    local_y = pressure.shape[2]
    depth_rows = pressure.shape[3]
    local_x = pressure.shape[4]
    depth_idx = lax.broadcasted_iota(jnp.int32, (1, depth_rows, 1), 1)
    floor_rows = seafloor[:, None, :]
    live = (depth_idx < floor_rows).astype(jnp.float32)
    bottom = (depth_idx == floor_rows - 1).astype(jnp.float32)
    above = (depth_idx < floor_rows - 1).astype(jnp.float32)
    rows_y = lax.broadcasted_iota(jnp.int32, (local_y, 1, 1), 0) + anchor_y
    cols_x = lax.broadcasted_iota(jnp.int32, (1, 1, local_x), 2) + anchor_x
    flat_cell = (depth_idx * total_y + rows_y) * total_x + cols_x
    source_hot = (flat_cell[None] == source_cell[:, None, None, None]).astype(jnp.float32)
    node_y = receiver_column // total_x
    node_x = receiver_column % total_x
    inside = (
        (node_y >= anchor_y)
        & (node_y < anchor_y + local_y)
        & (node_x >= anchor_x)
        & (node_x < anchor_x + local_x)
    )
    local_col = (node_y - anchor_y) * local_x + (node_x - anchor_x)
    column_iota = lax.broadcasted_iota(jnp.int32, (1, local_y * local_x), 1)
    node_hot = ((column_iota == local_col[:, None]) & inside[:, None]).astype(jnp.float32)
    grad_lambda = jnp.zeros(lame_lambda.shape, jnp.float32)
    grad_mu = jnp.zeros(lame_lambda.shape, jnp.float32)
    grad_kappa = jnp.zeros(water_kappa.shape, jnp.float32)
    misfits = []
    for step in range(wavelet.shape[0]):
        floor_pressure = jnp.sum(pressure * bottom, axis=3)
        stress_pad = solid_halo(jnp.stack([sig_xx, sig_xy, sig_xz]))
        vel_x = vel_x + TIME_STEP * solid_buoy * (
            stencil(stress_pad[0], 2, True) + derive(sig_xy, 4, False) + derive(sig_xz, 3, False)
        )
        vel_y = vel_y + TIME_STEP * solid_buoy * (
            stencil(stress_pad[1], 2, False) + derive(sig_yy, 4, True) + derive(sig_yz, 3, False)
        )
        vel_z = vel_z + TIME_STEP * solid_buoy * (
            stencil(stress_pad[2], 2, False) + derive(sig_yz, 4, False) + derive(sig_zz, 3, True)
        )
        floor_velocity = lax.all_to_all(
            jnp.transpose(vel_z[:, :, :, 0, :], (0, 1, 3, 2)),
            "gx",
            split_axis=2,
            concat_axis=3,
            tiled=True,
        )
        flow_x = (flow_x - TIME_STEP * water_buoy * water_derive(pressure, 4, True)) * live
        flow_y = (flow_y - TIME_STEP * water_buoy * water_derive(pressure, 2, True)) * live
        flow_z = (
            flow_z - TIME_STEP * water_buoy * derive(pressure, 3, True)
        ) * above + floor_velocity[:, :, :, None, :] * bottom
        velocity_pad = solid_halo(jnp.stack([vel_x, vel_y, vel_z]))
        strain_x = stencil(velocity_pad[0], 2, False)
        strain_y = derive(vel_y, 4, False)
        strain_z = derive(vel_z, 3, False)
        dilation = strain_x + strain_y + strain_z
        shear_xy = derive(vel_x, 4, True) + stencil(velocity_pad[1], 2, True)
        shear_xz = derive(vel_x, 3, True) + stencil(velocity_pad[2], 2, True)
        shear_yz = derive(vel_y, 3, True) + derive(vel_z, 4, True)
        lam_part = lame_lambda * dilation
        sig_xx = sig_xx + TIME_STEP * (lam_part + 2.0 * shear_mu * strain_x)
        sig_yy = sig_yy + TIME_STEP * (lam_part + 2.0 * shear_mu * strain_y)
        sig_zz = sig_zz + TIME_STEP * (lam_part + 2.0 * shear_mu * strain_z)
        sig_xy = sig_xy + TIME_STEP * shear_mu * shear_xy
        sig_xz = sig_xz + TIME_STEP * shear_mu * shear_xz
        sig_yz = sig_yz + TIME_STEP * shear_mu * shear_yz
        rock_pressure = jnp.transpose(
            lax.all_to_all(floor_pressure, "gx", split_axis=3, concat_axis=2, tiled=True),
            (0, 1, 3, 2),
        )
        sig_zz = sig_zz.at[:, :, :, 0, :].set(-rock_pressure)
        grad_lambda = grad_lambda + jnp.sum(dilation[0] * dilation[1], axis=0)
        normal_part = (
            strain_x[0] * strain_x[1] + strain_y[0] * strain_y[1] + strain_z[0] * strain_z[1]
        )
        shear_part = (
            shear_xy[0] * shear_xy[1] + shear_xz[0] * shear_xz[1] + shear_yz[0] * shear_yz[1]
        )
        grad_mu = grad_mu + jnp.sum(2.0 * normal_part + shear_part, axis=0)
        pressure = (
            pressure
            - TIME_STEP
            * water_kappa
            * (
                water_derive(flow_x, 4, False)
                + water_derive(flow_y, 2, False)
                + derive(flow_z, 3, False)
            )
        ) * live
        pressure = pressure.at[0].add(wavelet[step][:, None, None, None] * source_hot)
        surface = jnp.sum(pressure * bottom, axis=3)
        partial_record = jnp.einsum(
            "sc,rc->sr",
            surface[0].reshape(shots, local_y * local_x),
            node_hot,
            precision=lax.Precision.HIGHEST,
        )
        recorded = lax.psum(partial_record, "gx")
        misfit = recorded - observed[step]
        scaled = misfit * lax.rsqrt(jnp.mean(misfit * misfit, axis=1, keepdims=True) + 1e-06)
        inject = jnp.dot(
            scaled, node_hot, precision=lax.Precision.HIGHEST, preferred_element_type=jnp.float32
        ).reshape(shots, local_y, local_x)
        pressure = pressure.at[1].add(inject[:, :, None, :] * bottom)
        grad_kappa = grad_kappa + jnp.sum(pressure[0] * pressure[1], axis=0)
        misfits.append(misfit)
    return (grad_lambda, grad_mu, grad_kappa, jnp.stack(misfits))


def solution(mesh):
    placed = (
        P(None, None, "groups", "gx", None, None),
        P(None, None, "groups", "gx", None, None),
        P("gx", None, None),
        P("gx", None, None),
        P("gx", None, None),
        P("gx", None, None),
        P("gx", None, None),
        P("gx", None),
        P("groups"),
        P(None, "groups"),
        P(),
        P(None, "groups", None),
    )
    return jax.shard_map(
        on_device,
        mesh=mesh,
        in_specs=placed,
        out_specs=(
            P("gx", "groups", None),
            P("gx", "groups", None),
            P("gx", "groups", None),
            P(None, "groups", None),
        ),
        check_vma=False,
    )
```

profile of v0, /device:TPU:0, one launch (start us, length us, event | category | flops | bytes accessed | tf_op | source)
XLA Modules:
  0.0 367.0 jit_solution(11349562170741559003)
XLA Ops:
  2.9 3.0 collective-permute-start.11
  8.1 5.1 %collective-permute-start = (f32[3,2,1,4,4,128]{5,4,3,2,1,0:T(4,128)S(1)}, f32[3,2,1,4,4,128]{5,4,3,2,1,0:T(4,128)S(1)}, u32[]{:S(2)}, u32[]{:S(2)}) collective-permute-start(f32[3,2,1,4,4,128]{5,4,3,2,1,0:T(4,128)S(1)} %get-tuple-element.248), channel_id=1, source_target_pairs={{0,1},{1,2},{2,3},{3,4},{4,5},{5,6},{6,7},{7,8},{8,9},{9,10},{10,1... | collective-permute-start | bytes 147464 | tf_op jit(solution)/shard_map/ppermute | solution.py:17
  19.5 9.7 %all-to-all-start.1 = ((f32[2,1,128,8]{3,0,1,2:T(2,128)}), f32[2,1,128,8]{3,0,1,2:T(2,128)S(1)}, u32[]{:S(2)}, u32[]{:S(2)}) async-start(f32[2,1,128,8]{3,0,1,2:T(2,128)} %copy.963), calls=%async_computation.1 | async-start | bytes 262144 | tf_op jit(solution)/shard_map/all_to_all | solution.py:131
  31.2 3.0 collective-permute-start.2
  34.2 3.3 all-to-all-done.1
  40.4 3.0 collective-permute-start.4
  43.9 3.4 collective-permute-start.12
  52.6 12.4 %all-to-all-start = ((f32[2,1,4,256]{2,0,1,3:T(2,128)}), f32[2,1,4,256]{2,0,1,3:T(2,128)S(1)}, u32[]{:S(2)}, u32[]{:S(2)}) async-start(f32[2,1,4,256]{2,0,1,3:T(2,128)} %copy.948), calls=%async_computation | async-start | bytes 524288 | tf_op jit(solution)/shard_map/all_to_all | solution.py:159
  65.5 40.5 %psum.28 = f32[1,128]{1,0:T(1,128)S(1)} all-reduce(f32[1,128]{1,0:T(1,128)S(1)} %fusion.7), channel_id=1, replica_groups=mesh['groups'=1,'gx'=32] {'gx'}, use_global_device_ids=true, to_apply=%region_2.3 | all-reduce | flops 128 | bytes 1024 | tf_op jit(solution)/shard_map/psum | solution.py:189
  109.1 3.0 collective-permute-start.19
  113.6 6.2 %all-to-all-start.3 = ((f32[2,1,128,8]{3,0,1,2:T(2,128)}), f32[2,1,128,8]{3,0,1,2:T(2,128)S(1)}, u32[]{:S(2)}, u32[]{:S(2)}) async-start(f32[2,1,128,8]{3,0,1,2:T(2,128)} %copy.978), calls=%async_computation.3 | async-start | bytes 262144 | tf_op jit(solution)/shard_map/all_to_all | solution.py:131
  121.2 3.0 collective-permute-start.6
  124.2 3.8 %all-to-all-done.3 = f32[2,1,128,8]{3,0,1,2:T(2,128)S(1)} async-done(((f32[2,1,128,8]{3,0,1,2:T(2,128)}), f32[2,1,128,8]{3,0,1,2:T(2,128)S(1)}, u32[]{:S(2)}, u32[]{:S(2)}) %all-to-all-start.3) | async-done | bytes 8224 | tf_op jit(solution)/shard_map/all_to_all | solution.py:131
  130.4 3.0 collective-permute-start.8
  133.9 3.4 collective-permute-start.20
  142.7 11.9 %all-to-all-start.2 = ((f32[2,1,4,256]{2,0,1,3:T(2,128)}), f32[2,1,4,256]{2,0,1,3:T(2,128)S(1)}, u32[]{:S(2)}, u32[]{:S(2)}) async-start(f32[2,1,4,256]{2,0,1,3:T(2,128)} %copy.966), calls=%async_computation.2 | async-start | bytes 524288 | tf_op jit(solution)/shard_map/all_to_all | solution.py:159
  155.0 40.5 %psum.29 = f32[1,128]{1,0:T(1,128)S(1)} all-reduce(f32[1,128]{1,0:T(1,128)S(1)} %fusion.5), channel_id=1, replica_groups=mesh['groups'=1,'gx'=32] {'gx'}, use_global_device_ids=true, to_apply=%region_6.7 | all-reduce | flops 128 | bytes 1024 | tf_op jit(solution)/shard_map/psum | solution.py:189
  198.6 3.0 collective-permute-start.25
  203.1 6.2 %all-to-all-start.5 = ((f32[2,1,128,8]{3,0,1,2:T(2,128)}), f32[2,1,128,8]{3,0,1,2:T(2,128)S(1)}, u32[]{:S(2)}, u32[]{:S(2)}) async-start(f32[2,1,128,8]{3,0,1,2:T(2,128)} %copy.989), calls=%async_computation.5 | async-start | bytes 262144 | tf_op jit(solution)/shard_map/all_to_all | solution.py:131
  210.7 3.0 collective-permute-start.14
  213.7 3.8 %all-to-all-done.5 = f32[2,1,128,8]{3,0,1,2:T(2,128)S(1)} async-done(((f32[2,1,128,8]{3,0,1,2:T(2,128)}), f32[2,1,128,8]{3,0,1,2:T(2,128)S(1)}, u32[]{:S(2)}, u32[]{:S(2)}) %all-to-all-start.5) | async-done | bytes 8224 | tf_op jit(solution)/shard_map/all_to_all | solution.py:131
  219.9 3.0 collective-permute-start.16
  223.4 3.4 collective-permute-start.26
  232.2 11.9 %all-to-all-start.4 = ((f32[2,1,4,256]{2,0,1,3:T(2,128)}), f32[2,1,4,256]{2,0,1,3:T(2,128)S(1)}, u32[]{:S(2)}, u32[]{:S(2)}) async-start(f32[2,1,4,256]{2,0,1,3:T(2,128)} %copy.981), calls=%async_computation.4 | async-start | bytes 524288 | tf_op jit(solution)/shard_map/all_to_all | solution.py:159
  244.5 40.5 %psum.30 = f32[1,128]{1,0:T(1,128)S(1)} all-reduce(f32[1,128]{1,0:T(1,128)S(1)} %fusion.3), channel_id=1, replica_groups=mesh['groups'=1,'gx'=32] {'gx'}, use_global_device_ids=true, to_apply=%region_10.11 | all-reduce | flops 128 | bytes 1024 | tf_op jit(solution)/shard_map/psum | solution.py:189
  288.1 3.0 collective-permute-start.29
  292.6 6.2 %all-to-all-start.6 = ((f32[2,1,128,8]{3,0,1,2:T(2,128)}), f32[2,1,128,8]{3,0,1,2:T(2,128)S(1)}, u32[]{:S(2)}, u32[]{:S(2)}) async-start(f32[2,1,128,8]{3,0,1,2:T(2,128)} %copy.992), calls=%async_computation.6 | async-start | bytes 262144 | tf_op jit(solution)/shard_map/all_to_all | solution.py:131
  300.2 3.0 collective-permute-start.22
  303.2 3.8 %all-to-all-done.6 = f32[2,1,128,8]{3,0,1,2:T(2,128)S(1)} async-done(((f32[2,1,128,8]{3,0,1,2:T(2,128)}), f32[2,1,128,8]{3,0,1,2:T(2,128)S(1)}, u32[]{:S(2)}, u32[]{:S(2)}) %all-to-all-start.6) | async-done | bytes 8224 | tf_op jit(solution)/shard_map/all_to_all | solution.py:131
  309.1 2.1 collective-permute-start.30
  313.2 1.9 collective-permute-done.31
  316.8 46.5 %psum.31 = f32[1,128]{1,0:T(1,128)S(1)} all-reduce(f32[1,128]{1,0:T(1,128)S(1)} %fusion.1), channel_id=1, replica_groups=mesh['groups'=1,'gx'=32] {'gx'}, use_global_device_ids=true, to_apply=%region_13.14 | all-reduce | flops 128 | bytes 1024 | tf_op jit(solution)/shard_map/psum | solution.py:189
  (242 shorter events, 61.7 us)
Async XLA Ops:
  1.6 41.8 %collective-permute-start.10 = (f32[2,1,4,12,256]{4,2,3,1,0:T(4,128)S(1)}, f32[2,1,4,12,256]{4,2,3,1,0:T(4,128)S(1)}, u32[]{:S(2)}, u32[]{:S(2)}) collective-permute-start(f32[2,1,4,12,256]{4,2,3,1,0:T(4,128)S(1)} %slice_bitcast_fusion.3), channel_id=1, source_target_pairs={{1,0},{2,1},{3,2},{4,3},{5,4},{6,5},{7,6},{8,7},{9,8},{10,9},{11,1... | collective-permute-start | bytes 294920 | tf_op jit(solution)/shard_map/ppermute | solution.py:18
  2.9 40.5 %collective-permute-start.11 = (f32[2,1,4,12,256]{4,2,3,1,0:T(4,128)S(1)}, f32[2,1,4,12,256]{4,2,3,1,0:T(4,128)S(1)}, u32[]{:S(2)}, u32[]{:S(2)}) collective-permute-start(f32[2,1,4,12,256]{4,2,3,1,0:T(4,128)S(1)} %slice_bitcast_fusion.3), channel_id=1, source_target_pairs={{0,1},{1,2},{2,3},{3,4},{4,5},{5,6},{6,7},{7,8},{8,9},{9,10},{10,1... | collective-permute-start | bytes 294920 | tf_op jit(solution)/shard_map/ppermute | solution.py:17
  6.8 11.5 %collective-permute-start.1 = (f32[3,2,1,4,4,128]{5,4,3,2,1,0:T(4,128)S(1)}, f32[3,2,1,4,4,128]{5,4,3,2,1,0:T(4,128)S(1)}, u32[]{:S(2)}, u32[]{:S(2)}) collective-permute-start(f32[3,2,1,4,4,128]{5,4,3,2,1,0:T(4,128)S(1)} %get-tuple-element.249), channel_id=1, source_target_pairs={{1,0},{2,1},{3,2},{4,3},{5,4},{6,5},{7,6},{8,7},{9,8},{10,9},{11,1... | collective-permute-start | bytes 147464 | tf_op jit(solution)/shard_map/ppermute | solution.py:18
  8.1 10.3 %collective-permute-start = (f32[3,2,1,4,4,128]{5,4,3,2,1,0:T(4,128)S(1)}, f32[3,2,1,4,4,128]{5,4,3,2,1,0:T(4,128)S(1)}, u32[]{:S(2)}, u32[]{:S(2)}) collective-permute-start(f32[3,2,1,4,4,128]{5,4,3,2,1,0:T(4,128)S(1)} %get-tuple-element.248), channel_id=1, source_target_pairs={{0,1},{1,2},{2,3},{3,4},{4,5},{5,6},{6,7},{7,8},{8,9},{9,10},{10,1... | collective-permute-start | bytes 147464 | tf_op jit(solution)/shard_map/ppermute | solution.py:17
  19.5 18.0 %all-to-all-start.1 = ((f32[2,1,128,8]{3,0,1,2:T(2,128)}), f32[2,1,128,8]{3,0,1,2:T(2,128)S(1)}, u32[]{:S(2)}, u32[]{:S(2)}) async-start(f32[2,1,128,8]{3,0,1,2:T(2,128)} %copy.963), calls=%async_computation.1 | async-start | bytes 262144 | tf_op jit(solution)/shard_map/all_to_all | solution.py:131
  29.7 8.0 %collective-permute-start.3 = (f32[3,2,1,4,4,128]{5,4,3,2,1,0:T(4,128)S(1)}, f32[3,2,1,4,4,128]{5,4,3,2,1,0:T(4,128)S(1)}, u32[]{:S(2)}, u32[]{:S(2)}) collective-permute-start(f32[3,2,1,4,4,128]{5,4,3,2,1,0:T(4,128)S(1)} %get-tuple-element.247), channel_id=1, source_target_pairs={{1,0},{2,1},{3,2},{4,3},{5,4},{6,5},{7,6},{8,7},{9,8},{10,9},{11,1... | collective-permute-start | bytes 147464 | tf_op jit(solution)/shard_map/ppermute | solution.py:18
  31.2 6.6 %collective-permute-start.2 = (f32[3,2,1,4,4,128]{5,4,3,2,1,0:T(4,128)S(1)}, f32[3,2,1,4,4,128]{5,4,3,2,1,0:T(4,128)S(1)}, u32[]{:S(2)}, u32[]{:S(2)}) collective-permute-start(f32[3,2,1,4,4,128]{5,4,3,2,1,0:T(4,128)S(1)} %get-tuple-element.246), channel_id=1, source_target_pairs={{0,1},{1,2},{2,3},{3,4},{4,5},{5,6},{6,7},{7,8},{8,9},{9,10},{10,1... | collective-permute-start | bytes 147464 | tf_op jit(solution)/shard_map/ppermute | solution.py:17
  39.1 9.5 %collective-permute-start.5 = (f32[3,2,1,4,4,128]{5,4,3,2,1,0:T(4,128)S(1)}, f32[3,2,1,4,4,128]{5,4,3,2,1,0:T(4,128)S(1)}, u32[]{:S(2)}, u32[]{:S(2)}) collective-permute-start(f32[3,2,1,4,4,128]{5,4,3,2,1,0:T(4,128)S(1)} %get-tuple-element.245), channel_id=1, source_target_pairs={{1,0},{2,1},{3,2},{4,3},{5,4},{6,5},{7,6},{8,7},{9,8},{10,9},{11,1... | collective-permute-start | bytes 147464 | tf_op jit(solution)/shard_map/ppermute | solution.py:18
  40.4 8.2 %collective-permute-start.4 = (f32[3,2,1,4,4,128]{5,4,3,2,1,0:T(4,128)S(1)}, f32[3,2,1,4,4,128]{5,4,3,2,1,0:T(4,128)S(1)}, u32[]{:S(2)}, u32[]{:S(2)}) collective-permute-start(f32[3,2,1,4,4,128]{5,4,3,2,1,0:T(4,128)S(1)} %get-tuple-element.244), channel_id=1, source_target_pairs={{0,1},{1,2},{2,3},{3,4},{4,5},{5,6},{6,7},{7,8},{8,9},{9,10},{10,1... | collective-permute-start | bytes 147464 | tf_op jit(solution)/shard_map/ppermute | solution.py:17
  43.9 5.2 %collective-permute-start.12 = (f32[2,1,4,12,256]{4,2,3,1,0:T(4,128)S(1)}, f32[2,1,4,12,256]{4,2,3,1,0:T(4,128)S(1)}, u32[]{:S(2)}, u32[]{:S(2)}) collective-permute-start(f32[2,1,4,12,256]{4,2,3,1,0:T(4,128)S(1)} %get-tuple-element.190), channel_id=1, source_target_pairs={{0,1},{1,2},{2,3},{3,4},{4,5},{5,6},{6,7},{7,8},{8,9},{9,10},{10,1... | collective-permute-start | bytes 294920 | tf_op jit(solution)/shard_map/ppermute | solution.py:17
  52.6 59.5 %all-to-all-start = ((f32[2,1,4,256]{2,0,1,3:T(2,128)}), f32[2,1,4,256]{2,0,1,3:T(2,128)S(1)}, u32[]{:S(2)}, u32[]{:S(2)}) async-start(f32[2,1,4,256]{2,0,1,3:T(2,128)} %copy.948), calls=%async_computation | async-start | bytes 524288 | tf_op jit(solution)/shard_map/all_to_all | solution.py:159
  107.8 25.7 %collective-permute-start.18 = (f32[2,1,4,12,256]{4,2,3,1,0:T(4,128)S(1)}, f32[2,1,4,12,256]{4,2,3,1,0:T(4,128)S(1)}, u32[]{:S(2)}, u32[]{:S(2)}) collective-permute-start(f32[2,1,4,12,256]{4,2,3,1,0:T(4,128)S(1)} %fusion.1104), channel_id=1, source_target_pairs={{1,0},{2,1},{3,2},{4,3},{5,4},{6,5},{7,6},{8,7},{9,8},{10,9},{11,1... | collective-permute-start | bytes 294920 | tf_op jit(solution)/shard_map/ppermute | solution.py:18
  109.1 24.4 %collective-permute-start.19 = (f32[2,1,4,12,256]{4,2,3,1,0:T(4,128)S(1)}, f32[2,1,4,12,256]{4,2,3,1,0:T(4,128)S(1)}, u32[]{:S(2)}, u32[]{:S(2)}) collective-permute-start(f32[2,1,4,12,256]{4,2,3,1,0:T(4,128)S(1)} %fusion.1104), channel_id=1, source_target_pairs={{0,1},{1,2},{2,3},{3,4},{4,5},{5,6},{6,7},{7,8},{8,9},{9,10},{10,1... | collective-permute-start | bytes 294920 | tf_op jit(solution)/shard_map/ppermute | solution.py:17
  113.6 14.4 %all-to-all-start.3 = ((f32[2,1,128,8]{3,0,1,2:T(2,128)}), f32[2,1,128,8]{3,0,1,2:T(2,128)S(1)}, u32[]{:S(2)}, u32[]{:S(2)}) async-start(f32[2,1,128,8]{3,0,1,2:T(2,128)} %copy.978), calls=%async_computation.3 | async-start | bytes 262144 | tf_op jit(solution)/shard_map/all_to_all | solution.py:131
  119.9 8.4 %collective-permute-start.7 = (f32[3,2,1,4,4,128]{5,4,3,2,1,0:T(4,128)S(1)}, f32[3,2,1,4,4,128]{5,4,3,2,1,0:T(4,128)S(1)}, u32[]{:S(2)}, u32[]{:S(2)}) collective-permute-start(f32[3,2,1,4,4,128]{5,4,3,2,1,0:T(4,128)S(1)} %get-tuple-element.243), channel_id=1, source_target_pairs={{1,0},{2,1},{3,2},{4,3},{5,4},{6,5},{7,6},{8,7},{9,8},{10,9},{11,1... | collective-permute-start | bytes 147464 | tf_op jit(solution)/shard_map/ppermute | solution.py:18
  121.2 7.2 %collective-permute-start.6 = (f32[3,2,1,4,4,128]{5,4,3,2,1,0:T(4,128)S(1)}, f32[3,2,1,4,4,128]{5,4,3,2,1,0:T(4,128)S(1)}, u32[]{:S(2)}, u32[]{:S(2)}) collective-permute-start(f32[3,2,1,4,4,128]{5,4,3,2,1,0:T(4,128)S(1)} %get-tuple-element.242), channel_id=1, source_target_pairs={{0,1},{1,2},{2,3},{3,4},{4,5},{5,6},{6,7},{7,8},{8,9},{9,10},{10,1... | collective-permute-start | bytes 147464 | tf_op jit(solution)/shard_map/ppermute | solution.py:17
  129.1 9.5 %collective-permute-start.9 = (f32[3,2,1,4,4,128]{5,4,3,2,1,0:T(4,128)S(1)}, f32[3,2,1,4,4,128]{5,4,3,2,1,0:T(4,128)S(1)}, u32[]{:S(2)}, u32[]{:S(2)}) collective-permute-start(f32[3,2,1,4,4,128]{5,4,3,2,1,0:T(4,128)S(1)} %get-tuple-element.241), channel_id=1, source_target_pairs={{1,0},{2,1},{3,2},{4,3},{5,4},{6,5},{7,6},{8,7},{9,8},{10,9},{11,1... | collective-permute-start | bytes 147464 | tf_op jit(solution)/shard_map/ppermute | solution.py:18
  130.4 8.2 %collective-permute-start.8 = (f32[3,2,1,4,4,128]{5,4,3,2,1,0:T(4,128)S(1)}, f32[3,2,1,4,4,128]{5,4,3,2,1,0:T(4,128)S(1)}, u32[]{:S(2)}, u32[]{:S(2)}) collective-permute-start(f32[3,2,1,4,4,128]{5,4,3,2,1,0:T(4,128)S(1)} %get-tuple-element.240), channel_id=1, source_target_pairs={{0,1},{1,2},{2,3},{3,4},{4,5},{5,6},{6,7},{7,8},{8,9},{9,10},{10,1... | collective-permute-start | bytes 147464 | tf_op jit(solution)/shard_map/ppermute | solution.py:17
  142.7 59.0 %all-to-all-start.2 = ((f32[2,1,4,256]{2,0,1,3:T(2,128)}), f32[2,1,4,256]{2,0,1,3:T(2,128)S(1)}, u32[]{:S(2)}, u32[]{:S(2)}) async-start(f32[2,1,4,256]{2,0,1,3:T(2,128)} %copy.966), calls=%async_computation.2 | async-start | bytes 524288 | tf_op jit(solution)/shard_map/all_to_all | solution.py:159
  197.3 25.7 %collective-permute-start.24 = (f32[2,1,4,12,256]{4,2,3,1,0:T(4,128)S(1)}, f32[2,1,4,12,256]{4,2,3,1,0:T(4,128)S(1)}, u32[]{:S(2)}, u32[]{:S(2)}) collective-permute-start(f32[2,1,4,12,256]{4,2,3,1,0:T(4,128)S(1)} %fusion.1105), channel_id=1, source_target_pairs={{1,0},{2,1},{3,2},{4,3},{5,4},{6,5},{7,6},{8,7},{9,8},{10,9},{11,1... | collective-permute-start | bytes 294920 | tf_op jit(solution)/shard_map/ppermute | solution.py:18
  198.6 24.4 %collective-permute-start.25 = (f32[2,1,4,12,256]{4,2,3,1,0:T(4,128)S(1)}, f32[2,1,4,12,256]{4,2,3,1,0:T(4,128)S(1)}, u32[]{:S(2)}, u32[]{:S(2)}) collective-permute-start(f32[2,1,4,12,256]{4,2,3,1,0:T(4,128)S(1)} %fusion.1105), channel_id=1, source_target_pairs={{0,1},{1,2},{2,3},{3,4},{4,5},{5,6},{6,7},{7,8},{8,9},{9,10},{10,1... | collective-permute-start | bytes 294920 | tf_op jit(solution)/shard_map/ppermute | solution.py:17
  203.1 14.4 %all-to-all-start.5 = ((f32[2,1,128,8]{3,0,1,2:T(2,128)}), f32[2,1,128,8]{3,0,1,2:T(2,128)S(1)}, u32[]{:S(2)}, u32[]{:S(2)}) async-start(f32[2,1,128,8]{3,0,1,2:T(2,128)} %copy.989), calls=%async_computation.5 | async-start | bytes 262144 | tf_op jit(solution)/shard_map/all_to_all | solution.py:131
  209.4 8.4 %collective-permute-start.15 = (f32[3,2,1,4,4,128]{5,4,3,2,1,0:T(4,128)S(1)}, f32[3,2,1,4,4,128]{5,4,3,2,1,0:T(4,128)S(1)}, u32[]{:S(2)}, u32[]{:S(2)}) collective-permute-start(f32[3,2,1,4,4,128]{5,4,3,2,1,0:T(4,128)S(1)} %get-tuple-element.239), channel_id=1, source_target_pairs={{1,0},{2,1},{3,2},{4,3},{5,4},{6,5},{7,6},{8,7},{9,8},{10,9},{11,1... | collective-permute-start | bytes 147464 | tf_op jit(solution)/shard_map/ppermute | solution.py:18
  210.7 7.2 %collective-permute-start.14 = (f32[3,2,1,4,4,128]{5,4,3,2,1,0:T(4,128)S(1)}, f32[3,2,1,4,4,128]{5,4,3,2,1,0:T(4,128)S(1)}, u32[]{:S(2)}, u32[]{:S(2)}) collective-permute-start(f32[3,2,1,4,4,128]{5,4,3,2,1,0:T(4,128)S(1)} %get-tuple-element.238), channel_id=1, source_target_pairs={{0,1},{1,2},{2,3},{3,4},{4,5},{5,6},{6,7},{7,8},{8,9},{9,10},{10,1... | collective-permute-start | bytes 147464 | tf_op jit(solution)/shard_map/ppermute | solution.py:17
  218.6 9.5 %collective-permute-start.17 = (f32[3,2,1,4,4,128]{5,4,3,2,1,0:T(4,128)S(1)}, f32[3,2,1,4,4,128]{5,4,3,2,1,0:T(4,128)S(1)}, u32[]{:S(2)}, u32[]{:S(2)}) collective-permute-start(f32[3,2,1,4,4,128]{5,4,3,2,1,0:T(4,128)S(1)} %get-tuple-element.237), channel_id=1, source_target_pairs={{1,0},{2,1},{3,2},{4,3},{5,4},{6,5},{7,6},{8,7},{9,8},{10,9},{11,1... | collective-permute-start | bytes 147464 | tf_op jit(solution)/shard_map/ppermute | solution.py:18
  219.9 8.2 %collective-permute-start.16 = (f32[3,2,1,4,4,128]{5,4,3,2,1,0:T(4,128)S(1)}, f32[3,2,1,4,4,128]{5,4,3,2,1,0:T(4,128)S(1)}, u32[]{:S(2)}, u32[]{:S(2)}) collective-permute-start(f32[3,2,1,4,4,128]{5,4,3,2,1,0:T(4,128)S(1)} %get-tuple-element.236), channel_id=1, source_target_pairs={{0,1},{1,2},{2,3},{3,4},{4,5},{5,6},{6,7},{7,8},{8,9},{9,10},{10,1... | collective-permute-start | bytes 147464 | tf_op jit(solution)/shard_map/ppermute | solution.py:17
  232.2 59.0 %all-to-all-start.4 = ((f32[2,1,4,256]{2,0,1,3:T(2,128)}), f32[2,1,4,256]{2,0,1,3:T(2,128)S(1)}, u32[]{:S(2)}, u32[]{:S(2)}) async-start(f32[2,1,4,256]{2,0,1,3:T(2,128)} %copy.981), calls=%async_computation.4 | async-start | bytes 524288 | tf_op jit(solution)/shard_map/all_to_all | solution.py:159
  286.8 21.9 %collective-permute-start.28 = (f32[2,1,4,12,256]{4,2,3,1,0:T(4,128)S(1)}, f32[2,1,4,12,256]{4,2,3,1,0:T(4,128)S(1)}, u32[]{:S(2)}, u32[]{:S(2)}) collective-permute-start(f32[2,1,4,12,256]{4,2,3,1,0:T(4,128)S(1)} %fusion.1106), channel_id=1, source_target_pairs={{1,0},{2,1},{3,2},{4,3},{5,4},{6,5},{7,6},{8,7},{9,8},{10,9},{11,1... | collective-permute-start | bytes 294920 | tf_op jit(solution)/shard_map/ppermute | solution.py:18
  288.1 20.6 %collective-permute-start.29 = (f32[2,1,4,12,256]{4,2,3,1,0:T(4,128)S(1)}, f32[2,1,4,12,256]{4,2,3,1,0:T(4,128)S(1)}, u32[]{:S(2)}, u32[]{:S(2)}) collective-permute-start(f32[2,1,4,12,256]{4,2,3,1,0:T(4,128)S(1)} %fusion.1106), channel_id=1, source_target_pairs={{0,1},{1,2},{2,3},{3,4},{4,5},{5,6},{6,7},{7,8},{8,9},{9,10},{10,1... | collective-permute-start | bytes 294920 | tf_op jit(solution)/shard_map/ppermute | solution.py:17
  292.6 14.4 %all-to-all-start.6 = ((f32[2,1,128,8]{3,0,1,2:T(2,128)}), f32[2,1,128,8]{3,0,1,2:T(2,128)S(1)}, u32[]{:S(2)}, u32[]{:S(2)}) async-start(f32[2,1,128,8]{3,0,1,2:T(2,128)} %copy.992), calls=%async_computation.6 | async-start | bytes 262144 | tf_op jit(solution)/shard_map/all_to_all | solution.py:131
  298.9 8.4 %collective-permute-start.23 = (f32[3,2,1,4,4,128]{5,4,3,2,1,0:T(4,128)S(1)}, f32[3,2,1,4,4,128]{5,4,3,2,1,0:T(4,128)S(1)}, u32[]{:S(2)}, u32[]{:S(2)}) collective-permute-start(f32[3,2,1,4,4,128]{5,4,3,2,1,0:T(4,128)S(1)} %get-tuple-element.235), channel_id=1, source_target_pairs={{1,0},{2,1},{3,2},{4,3},{5,4},{6,5},{7,6},{8,7},{9,8},{10,9},{11,1... | collective-permute-start | bytes 147464 | tf_op jit(solution)/shard_map/ppermute | solution.py:18
  300.2 7.2 %collective-permute-start.22 = (f32[3,2,1,4,4,128]{5,4,3,2,1,0:T(4,128)S(1)}, f32[3,2,1,4,4,128]{5,4,3,2,1,0:T(4,128)S(1)}, u32[]{:S(2)}, u32[]{:S(2)}) collective-permute-start(f32[3,2,1,4,4,128]{5,4,3,2,1,0:T(4,128)S(1)} %get-tuple-element.234), channel_id=1, source_target_pairs={{0,1},{1,2},{2,3},{3,4},{4,5},{5,6},{6,7},{7,8},{8,9},{9,10},{10,1... | collective-permute-start | bytes 147464 | tf_op jit(solution)/shard_map/ppermute | solution.py:17
  (18 other events, 94.4 us)
where the time goes:
time: 369 us; the launch traced here: 367 us
  blocking collectives  168 us (46%)
  starting transfers between devices  136 us (37%)
  waiting for transfers between devices  21 us (6%)
  other arithmetic  18.8 us (5%)
  local copies, waits for them, and re-layouts  14.5 us (4%)
  between operations  5.44 us (1%)
    psum x4, blocking collectives, on_device(): recorded = lax.psum(partial_record, 'gx')  168 us
    ppermute x16, starting transfers between devices, with_halo(): before = lax.ppermute(last, axis, up)  50.7 us
    all_to_all x3, starting transfers between devices, on_device(): lax.all_to_all(floor_pressure, 'gx', split_axis=3, concat_axis=2, tiled=T...  36.3 us
    all_to_all x4, starting transfers between devices, on_device(): lax.all_to_all(jnp.transpose(vel_z[:, :, :, 0, :], (0, 1, 3, 2)), 'gx', s...  28.3 us
    ppermute x16, starting transfers between devices, with_halo(): after = lax.ppermute(first, axis, down)  20.8 us
    all_to_all x4, waiting for transfers between devices, on_device(): lax.all_to_all(jnp.transpose(vel_z[:, :, :, 0, :], (0, 1, 3, 2)), 'gx', s...  14.8 us
  transfers between devices with their start and end apart: 39, of which 8 were waited for; matrix products, arithmetic and copies ran while one was open for 5% of the time, Pallas kernels for 0%

commit v1 on v0

--- a/solution.py
+++ b/solution.py
@@ -186,7 +186,7 @@
             node_hot,
             precision=lax.Precision.HIGHEST,
         )
-        recorded = lax.psum(partial_record, "gx")
+        recorded = jnp.sum(lax.all_gather(partial_record, "gx"), 0)
         misfit = recorded - observed[step]
         scaled = misfit * lax.rsqrt(jnp.mean(misfit * misfit, axis=1, keepdims=True) + 1e-06)
         inject = jnp.dot(

time: 369 us -> 351 us (0.951)
  starting transfers between devices: 136 us -> 96.9 us
  waiting for transfers between devices: 21 us -> 36 us
  blocking collectives: 168 us -> 174 us
    all_gather x0 -> x4, blocking collectives: none -> 174 us  [on_device(): recorded = jnp.sum(lax.all_gather(partial_record, 'gx'), 0)]
    psum x4 -> x0, blocking collectives: 168 us -> none  [on_device(): recorded = lax.psum(partial_record, 'gx')]
    all_to_all x3, starting transfers between devices: 36.3 us -> 7.75 us  [on_device(): lax.all_to_all(floor_pressure, 'gx', split_axis=3, concat_axis=2, tiled=T...]
    all_to_all x3, waiting for transfers between devices: 0.01 us -> 15.2 us  [on_device(): lax.all_to_all(floor_pressure, 'gx', split_axis=3, concat_axis=2, tiled=T...]
    all_to_all x4, starting transfers between devices: 28.3 us -> 17.5 us  [on_device(): lax.all_to_all(jnp.transpose(vel_z[:, :, :, 0, :], (0, 1, 3, 2)), 'gx', s...]
  transfers between devices with their start and end apart: 39 -> 39, of which waited for: 8 -> 11; matrix products, arithmetic and copies ran while one was open for 5% -> 5% of each run, Pallas kernels for 0% -> 0%
where the time goes in v1:
time: 351 us; the launch traced here: 349 us
  blocking collectives  174 us (50%)
  starting transfers between devices  96.9 us (28%)
  waiting for transfers between devices  36 us (10%)
  other arithmetic  19 us (5%)
  local copies, waits for them, and re-layouts  15.1 us (4%)
  between operations  5.4 us (2%)
    all_gather x4, blocking collectives, on_device(): recorded = jnp.sum(lax.all_gather(partial_record, 'gx'), 0)  174 us
    ppermute x16, starting transfers between devices, with_halo(): before = lax.ppermute(last, axis, up)  50.9 us
    ppermute x16, starting transfers between devices, with_halo(): after = lax.ppermute(first, axis, down)  20.8 us
    all_to_all x4, starting transfers between devices, on_device(): lax.all_to_all(jnp.transpose(vel_z[:, :, :, 0, :], (0, 1, 3, 2)), 'gx', s...  17.5 us
    all_to_all x3, waiting for transfers between devices, on_device(): lax.all_to_all(floor_pressure, 'gx', split_axis=3, concat_axis=2, tiled=T...  15.2 us
    all_to_all x4, waiting for transfers between devices, on_device(): lax.all_to_all(jnp.transpose(vel_z[:, :, :, 0, :], (0, 1, 3, 2)), 'gx', s...  14.6 us
    all_to_all x3, starting transfers between devices, on_device(): lax.all_to_all(floor_pressure, 'gx', split_axis=3, concat_axis=2, tiled=T...  7.75 us
  transfers between devices with their start and end apart: 39, of which 11 were waited for; matrix products, arithmetic and copies ran while one was open for 5% of the time, Pallas kernels for 0%

profile of v1, /device:TPU:0, one launch (start us, length us, event | category | flops | bytes accessed | tf_op | source)
XLA Modules:
  0.0 349.3 jit_solution(11933936070988885286)
XLA Ops:
  2.9 3.0 collective-permute-start.11
  8.1 5.1 %collective-permute-start = (f32[3,2,1,4,4,128]{5,4,3,2,1,0:T(4,128)S(1)}, f32[3,2,1,4,4,128]{5,4,3,2,1,0:T(4,128)S(1)}, u32[]{:S(2)}, u32[]{:S(2)}) collective-permute-start(f32[3,2,1,4,4,128]{5,4,3,2,1,0:T(4,128)S(1)} %get-tuple-element.248), channel_id=1, source_target_pairs={{0,1},{1,2},{2,3},{3,4},{4,5},{5,6},{6,7},{7,8},{8,9},{9,10},{10,1... | collective-permute-start | bytes 147464 | tf_op jit(solution)/shard_map/ppermute | solution.py:17
  19.5 9.7 %all-to-all-start.1 = ((f32[2,1,128,8]{3,0,1,2:T(2,128)}), f32[2,1,128,8]{3,0,1,2:T(2,128)S(1)}, u32[]{:S(2)}, u32[]{:S(2)}) async-start(f32[2,1,128,8]{3,0,1,2:T(2,128)} %copy.963), calls=%async_computation.1 | async-start | bytes 262144 | tf_op jit(solution)/shard_map/all_to_all | solution.py:131
  31.2 3.0 collective-permute-start.2
  34.2 3.3 all-to-all-done.1
  40.4 3.0 collective-permute-start.4
  43.9 3.4 collective-permute-start.12
  52.2 43.7 %all-gather.4 = f32[32,1,128]{2,1,0:T(1,128)S(1)} all-gather(f32[1,1,128]{2,1,0:T(1,128)S(1)} %convolution_bitcast_fusion.3), channel_id=2, replica_groups=mesh['groups'=1,'gx'=32] {'gx'}, dimensions={0}, use_global_device_ids=true | all-gather | bytes 16896 | tf_op jit(solution)/shard_map/all_gather | solution.py:189
  98.0 2.6 all-to-all-start
  103.1 3.0 collective-permute-start.19
  106.2 5.1 %all-to-all-done = f32[2,1,4,256]{2,0,1,3:T(2,128)S(1)} async-done(((f32[2,1,4,256]{2,0,1,3:T(2,128)}), f32[2,1,4,256]{2,0,1,3:T(2,128)S(1)}, u32[]{:S(2)}, u32[]{:S(2)}) %all-to-all-start) | async-done | bytes 8224 | tf_op jit(solution)/shard_map/all_to_all | solution.py:159
  112.7 2.6 all-to-all-start.3
  116.7 3.0 collective-permute-start.6
  119.7 3.8 %all-to-all-done.3 = f32[2,1,128,8]{3,0,1,2:T(2,128)S(1)} async-done(((f32[2,1,128,8]{3,0,1,2:T(2,128)}), f32[2,1,128,8]{3,0,1,2:T(2,128)S(1)}, u32[]{:S(2)}, u32[]{:S(2)}) %all-to-all-start.3) | async-done | bytes 8224 | tf_op jit(solution)/shard_map/all_to_all | solution.py:131
  125.9 3.0 collective-permute-start.8
  129.4 3.4 collective-permute-start.20
  137.7 43.2 %all-gather.5 = f32[32,1,128]{2,1,0:T(1,128)S(1)} all-gather(f32[1,1,128]{2,1,0:T(1,128)S(1)} %convolution_bitcast_fusion.2), channel_id=3, replica_groups=mesh['groups'=1,'gx'=32] {'gx'}, dimensions={0}, use_global_device_ids=true | all-gather | bytes 16896 | tf_op jit(solution)/shard_map/all_gather | solution.py:189
  182.4 2.6 all-to-all-start.2
  187.5 3.0 collective-permute-start.25
  190.5 5.1 %all-to-all-done.2 = f32[2,1,4,256]{2,0,1,3:T(2,128)S(1)} async-done(((f32[2,1,4,256]{2,0,1,3:T(2,128)}), f32[2,1,4,256]{2,0,1,3:T(2,128)S(1)}, u32[]{:S(2)}, u32[]{:S(2)}) %all-to-all-start.2) | async-done | bytes 8224 | tf_op jit(solution)/shard_map/all_to_all | solution.py:159
  197.1 2.6 all-to-all-start.5
  201.0 3.2 collective-permute-start.14
  204.3 3.7 %all-to-all-done.5 = f32[2,1,128,8]{3,0,1,2:T(2,128)S(1)} async-done(((f32[2,1,128,8]{3,0,1,2:T(2,128)}), f32[2,1,128,8]{3,0,1,2:T(2,128)S(1)}, u32[]{:S(2)}, u32[]{:S(2)}) %all-to-all-start.5) | async-done | bytes 8224 | tf_op jit(solution)/shard_map/all_to_all | solution.py:131
  210.3 3.0 collective-permute-start.16
  213.8 3.4 collective-permute-start.26
  222.1 43.2 %all-gather.6 = f32[32,1,128]{2,1,0:T(1,128)S(1)} all-gather(f32[1,1,128]{2,1,0:T(1,128)S(1)} %convolution_bitcast_fusion.1), channel_id=4, replica_groups=mesh['groups'=1,'gx'=32] {'gx'}, dimensions={0}, use_global_device_ids=true | all-gather | bytes 16896 | tf_op jit(solution)/shard_map/all_gather | solution.py:189
  271.9 3.0 collective-permute-start.29
  274.9 5.1 %all-to-all-done.4 = f32[2,1,4,256]{2,0,1,3:T(2,128)S(1)} async-done(((f32[2,1,4,256]{2,0,1,3:T(2,128)}), f32[2,1,4,256]{2,0,1,3:T(2,128)S(1)}, u32[]{:S(2)}, u32[]{:S(2)}) %all-to-all-start.4) | async-done | bytes 8224 | tf_op jit(solution)/shard_map/all_to_all | solution.py:159
  281.5 2.6 all-to-all-start.6
  285.4 3.0 collective-permute-start.22
  288.5 3.8 %all-to-all-done.6 = f32[2,1,128,8]{3,0,1,2:T(2,128)S(1)} async-done(((f32[2,1,128,8]{3,0,1,2:T(2,128)}), f32[2,1,128,8]{3,0,1,2:T(2,128)S(1)}, u32[]{:S(2)}, u32[]{:S(2)}) %all-to-all-start.6) | async-done | bytes 8224 | tf_op jit(solution)/shard_map/all_to_all | solution.py:131
  302.1 43.5 %all-gather.7 = f32[32,1,128]{2,1,0:T(1,128)S(1)} all-gather(f32[1,1,128]{2,1,0:T(1,128)S(1)} %convolution_bitcast_fusion), channel_id=5, replica_groups=mesh['groups'=1,'gx'=32] {'gx'}, dimensions={0}, use_global_device_ids=true | all-gather | bytes 16896 | tf_op jit(solution)/shard_map/all_gather | solution.py:189
  (250 shorter events, 69.1 us)
Async XLA Ops:
  1.6 41.8 %collective-permute-start.10 = (f32[2,1,4,12,256]{4,2,3,1,0:T(4,128)S(1)}, f32[2,1,4,12,256]{4,2,3,1,0:T(4,128)S(1)}, u32[]{:S(2)}, u32[]{:S(2)}) collective-permute-start(f32[2,1,4,12,256]{4,2,3,1,0:T(4,128)S(1)} %slice_bitcast_fusion.3), channel_id=1, source_target_pairs={{1,0},{2,1},{3,2},{4,3},{5,4},{6,5},{7,6},{8,7},{9,8},{10,9},{11,1... | collective-permute-start | bytes 294920 | tf_op jit(solution)/shard_map/ppermute | solution.py:18
  2.9 40.5 %collective-permute-start.11 = (f32[2,1,4,12,256]{4,2,3,1,0:T(4,128)S(1)}, f32[2,1,4,12,256]{4,2,3,1,0:T(4,128)S(1)}, u32[]{:S(2)}, u32[]{:S(2)}) collective-permute-start(f32[2,1,4,12,256]{4,2,3,1,0:T(4,128)S(1)} %slice_bitcast_fusion.3), channel_id=1, source_target_pairs={{0,1},{1,2},{2,3},{3,4},{4,5},{5,6},{6,7},{7,8},{8,9},{9,10},{10,1... | collective-permute-start | bytes 294920 | tf_op jit(solution)/shard_map/ppermute | solution.py:17
  6.8 11.5 %collective-permute-start.1 = (f32[3,2,1,4,4,128]{5,4,3,2,1,0:T(4,128)S(1)}, f32[3,2,1,4,4,128]{5,4,3,2,1,0:T(4,128)S(1)}, u32[]{:S(2)}, u32[]{:S(2)}) collective-permute-start(f32[3,2,1,4,4,128]{5,4,3,2,1,0:T(4,128)S(1)} %get-tuple-element.249), channel_id=1, source_target_pairs={{1,0},{2,1},{3,2},{4,3},{5,4},{6,5},{7,6},{8,7},{9,8},{10,9},{11,1... | collective-permute-start | bytes 147464 | tf_op jit(solution)/shard_map/ppermute | solution.py:18
  8.1 10.3 %collective-permute-start = (f32[3,2,1,4,4,128]{5,4,3,2,1,0:T(4,128)S(1)}, f32[3,2,1,4,4,128]{5,4,3,2,1,0:T(4,128)S(1)}, u32[]{:S(2)}, u32[]{:S(2)}) collective-permute-start(f32[3,2,1,4,4,128]{5,4,3,2,1,0:T(4,128)S(1)} %get-tuple-element.248), channel_id=1, source_target_pairs={{0,1},{1,2},{2,3},{3,4},{4,5},{5,6},{6,7},{7,8},{8,9},{9,10},{10,1... | collective-permute-start | bytes 147464 | tf_op jit(solution)/shard_map/ppermute | solution.py:17
  19.5 18.0 %all-to-all-start.1 = ((f32[2,1,128,8]{3,0,1,2:T(2,128)}), f32[2,1,128,8]{3,0,1,2:T(2,128)S(1)}, u32[]{:S(2)}, u32[]{:S(2)}) async-start(f32[2,1,128,8]{3,0,1,2:T(2,128)} %copy.963), calls=%async_computation.1 | async-start | bytes 262144 | tf_op jit(solution)/shard_map/all_to_all | solution.py:131
  29.7 8.0 %collective-permute-start.3 = (f32[3,2,1,4,4,128]{5,4,3,2,1,0:T(4,128)S(1)}, f32[3,2,1,4,4,128]{5,4,3,2,1,0:T(4,128)S(1)}, u32[]{:S(2)}, u32[]{:S(2)}) collective-permute-start(f32[3,2,1,4,4,128]{5,4,3,2,1,0:T(4,128)S(1)} %get-tuple-element.247), channel_id=1, source_target_pairs={{1,0},{2,1},{3,2},{4,3},{5,4},{6,5},{7,6},{8,7},{9,8},{10,9},{11,1... | collective-permute-start | bytes 147464 | tf_op jit(solution)/shard_map/ppermute | solution.py:18
  31.2 6.6 %collective-permute-start.2 = (f32[3,2,1,4,4,128]{5,4,3,2,1,0:T(4,128)S(1)}, f32[3,2,1,4,4,128]{5,4,3,2,1,0:T(4,128)S(1)}, u32[]{:S(2)}, u32[]{:S(2)}) collective-permute-start(f32[3,2,1,4,4,128]{5,4,3,2,1,0:T(4,128)S(1)} %get-tuple-element.246), channel_id=1, source_target_pairs={{0,1},{1,2},{2,3},{3,4},{4,5},{5,6},{6,7},{7,8},{8,9},{9,10},{10,1... | collective-permute-start | bytes 147464 | tf_op jit(solution)/shard_map/ppermute | solution.py:17
  39.1 9.5 %collective-permute-start.5 = (f32[3,2,1,4,4,128]{5,4,3,2,1,0:T(4,128)S(1)}, f32[3,2,1,4,4,128]{5,4,3,2,1,0:T(4,128)S(1)}, u32[]{:S(2)}, u32[]{:S(2)}) collective-permute-start(f32[3,2,1,4,4,128]{5,4,3,2,1,0:T(4,128)S(1)} %get-tuple-element.245), channel_id=1, source_target_pairs={{1,0},{2,1},{3,2},{4,3},{5,4},{6,5},{7,6},{8,7},{9,8},{10,9},{11,1... | collective-permute-start | bytes 147464 | tf_op jit(solution)/shard_map/ppermute | solution.py:18
  40.4 8.2 %collective-permute-start.4 = (f32[3,2,1,4,4,128]{5,4,3,2,1,0:T(4,128)S(1)}, f32[3,2,1,4,4,128]{5,4,3,2,1,0:T(4,128)S(1)}, u32[]{:S(2)}, u32[]{:S(2)}) collective-permute-start(f32[3,2,1,4,4,128]{5,4,3,2,1,0:T(4,128)S(1)} %get-tuple-element.244), channel_id=1, source_target_pairs={{0,1},{1,2},{2,3},{3,4},{4,5},{5,6},{6,7},{7,8},{8,9},{9,10},{10,1... | collective-permute-start | bytes 147464 | tf_op jit(solution)/shard_map/ppermute | solution.py:17
  43.9 5.2 %collective-permute-start.12 = (f32[2,1,4,12,256]{4,2,3,1,0:T(4,128)S(1)}, f32[2,1,4,12,256]{4,2,3,1,0:T(4,128)S(1)}, u32[]{:S(2)}, u32[]{:S(2)}) collective-permute-start(f32[2,1,4,12,256]{4,2,3,1,0:T(4,128)S(1)} %get-tuple-element.190), channel_id=1, source_target_pairs={{0,1},{1,2},{2,3},{3,4},{4,5},{5,6},{6,7},{7,8},{8,9},{9,10},{10,1... | collective-permute-start | bytes 294920 | tf_op jit(solution)/shard_map/ppermute | solution.py:17
  98.0 13.2 %all-to-all-start = ((f32[2,1,4,256]{2,0,1,3:T(2,128)}), f32[2,1,4,256]{2,0,1,3:T(2,128)S(1)}, u32[]{:S(2)}, u32[]{:S(2)}) async-start(f32[2,1,4,256]{2,0,1,3:T(2,128)} %copy.948), calls=%async_computation | async-start | bytes 524288 | tf_op jit(solution)/shard_map/all_to_all | solution.py:159
  101.8 27.1 %collective-permute-start.18 = (f32[2,1,4,12,256]{4,2,3,1,0:T(4,128)S(1)}, f32[2,1,4,12,256]{4,2,3,1,0:T(4,128)S(1)}, u32[]{:S(2)}, u32[]{:S(2)}) collective-permute-start(f32[2,1,4,12,256]{4,2,3,1,0:T(4,128)S(1)} %fusion.1100), channel_id=1, source_target_pairs={{1,0},{2,1},{3,2},{4,3},{5,4},{6,5},{7,6},{8,7},{9,8},{10,9},{11,1... | collective-permute-start | bytes 294920 | tf_op jit(solution)/shard_map/ppermute | solution.py:18
  103.1 25.8 %collective-permute-start.19 = (f32[2,1,4,12,256]{4,2,3,1,0:T(4,128)S(1)}, f32[2,1,4,12,256]{4,2,3,1,0:T(4,128)S(1)}, u32[]{:S(2)}, u32[]{:S(2)}) collective-permute-start(f32[2,1,4,12,256]{4,2,3,1,0:T(4,128)S(1)} %fusion.1100), channel_id=1, source_target_pairs={{0,1},{1,2},{2,3},{3,4},{4,5},{5,6},{6,7},{7,8},{8,9},{9,10},{10,1... | collective-permute-start | bytes 294920 | tf_op jit(solution)/shard_map/ppermute | solution.py:17
  112.7 10.8 %all-to-all-start.3 = ((f32[2,1,128,8]{3,0,1,2:T(2,128)}), f32[2,1,128,8]{3,0,1,2:T(2,128)S(1)}, u32[]{:S(2)}, u32[]{:S(2)}) async-start(f32[2,1,128,8]{3,0,1,2:T(2,128)} %copy.978), calls=%async_computation.3 | async-start | bytes 262144 | tf_op jit(solution)/shard_map/all_to_all | solution.py:131
  115.4 8.4 %collective-permute-start.7 = (f32[3,2,1,4,4,128]{5,4,3,2,1,0:T(4,128)S(1)}, f32[3,2,1,4,4,128]{5,4,3,2,1,0:T(4,128)S(1)}, u32[]{:S(2)}, u32[]{:S(2)}) collective-permute-start(f32[3,2,1,4,4,128]{5,4,3,2,1,0:T(4,128)S(1)} %get-tuple-element.243), channel_id=1, source_target_pairs={{1,0},{2,1},{3,2},{4,3},{5,4},{6,5},{7,6},{8,7},{9,8},{10,9},{11,1... | collective-permute-start | bytes 147464 | tf_op jit(solution)/shard_map/ppermute | solution.py:18
  116.7 7.2 %collective-permute-start.6 = (f32[3,2,1,4,4,128]{5,4,3,2,1,0:T(4,128)S(1)}, f32[3,2,1,4,4,128]{5,4,3,2,1,0:T(4,128)S(1)}, u32[]{:S(2)}, u32[]{:S(2)}) collective-permute-start(f32[3,2,1,4,4,128]{5,4,3,2,1,0:T(4,128)S(1)} %get-tuple-element.242), channel_id=1, source_target_pairs={{0,1},{1,2},{2,3},{3,4},{4,5},{5,6},{6,7},{7,8},{8,9},{9,10},{10,1... | collective-permute-start | bytes 147464 | tf_op jit(solution)/shard_map/ppermute | solution.py:17
  124.6 9.5 %collective-permute-start.9 = (f32[3,2,1,4,4,128]{5,4,3,2,1,0:T(4,128)S(1)}, f32[3,2,1,4,4,128]{5,4,3,2,1,0:T(4,128)S(1)}, u32[]{:S(2)}, u32[]{:S(2)}) collective-permute-start(f32[3,2,1,4,4,128]{5,4,3,2,1,0:T(4,128)S(1)} %get-tuple-element.241), channel_id=1, source_target_pairs={{1,0},{2,1},{3,2},{4,3},{5,4},{6,5},{7,6},{8,7},{9,8},{10,9},{11,1... | collective-permute-start | bytes 147464 | tf_op jit(solution)/shard_map/ppermute | solution.py:18
  125.9 8.2 %collective-permute-start.8 = (f32[3,2,1,4,4,128]{5,4,3,2,1,0:T(4,128)S(1)}, f32[3,2,1,4,4,128]{5,4,3,2,1,0:T(4,128)S(1)}, u32[]{:S(2)}, u32[]{:S(2)}) collective-permute-start(f32[3,2,1,4,4,128]{5,4,3,2,1,0:T(4,128)S(1)} %get-tuple-element.240), channel_id=1, source_target_pairs={{0,1},{1,2},{2,3},{3,4},{4,5},{5,6},{6,7},{7,8},{8,9},{9,10},{10,1... | collective-permute-start | bytes 147464 | tf_op jit(solution)/shard_map/ppermute | solution.py:17
  182.4 13.2 %all-to-all-start.2 = ((f32[2,1,4,256]{2,0,1,3:T(2,128)}), f32[2,1,4,256]{2,0,1,3:T(2,128)S(1)}, u32[]{:S(2)}, u32[]{:S(2)}) async-start(f32[2,1,4,256]{2,0,1,3:T(2,128)} %copy.966), calls=%async_computation.2 | async-start | bytes 524288 | tf_op jit(solution)/shard_map/all_to_all | solution.py:159
  186.2 27.1 %collective-permute-start.24 = (f32[2,1,4,12,256]{4,2,3,1,0:T(4,128)S(1)}, f32[2,1,4,12,256]{4,2,3,1,0:T(4,128)S(1)}, u32[]{:S(2)}, u32[]{:S(2)}) collective-permute-start(f32[2,1,4,12,256]{4,2,3,1,0:T(4,128)S(1)} %fusion.1101), channel_id=1, source_target_pairs={{1,0},{2,1},{3,2},{4,3},{5,4},{6,5},{7,6},{8,7},{9,8},{10,9},{11,1... | collective-permute-start | bytes 294920 | tf_op jit(solution)/shard_map/ppermute | solution.py:18
  187.5 25.8 %collective-permute-start.25 = (f32[2,1,4,12,256]{4,2,3,1,0:T(4,128)S(1)}, f32[2,1,4,12,256]{4,2,3,1,0:T(4,128)S(1)}, u32[]{:S(2)}, u32[]{:S(2)}) collective-permute-start(f32[2,1,4,12,256]{4,2,3,1,0:T(4,128)S(1)} %fusion.1101), channel_id=1, source_target_pairs={{0,1},{1,2},{2,3},{3,4},{4,5},{5,6},{6,7},{7,8},{8,9},{9,10},{10,1... | collective-permute-start | bytes 294920 | tf_op jit(solution)/shard_map/ppermute | solution.py:17
  197.1 10.8 %all-to-all-start.5 = ((f32[2,1,128,8]{3,0,1,2:T(2,128)}), f32[2,1,128,8]{3,0,1,2:T(2,128)S(1)}, u32[]{:S(2)}, u32[]{:S(2)}) async-start(f32[2,1,128,8]{3,0,1,2:T(2,128)} %copy.989), calls=%async_computation.5 | async-start | bytes 262144 | tf_op jit(solution)/shard_map/all_to_all | solution.py:131
  199.7 8.4 %collective-permute-start.15 = (f32[3,2,1,4,4,128]{5,4,3,2,1,0:T(4,128)S(1)}, f32[3,2,1,4,4,128]{5,4,3,2,1,0:T(4,128)S(1)}, u32[]{:S(2)}, u32[]{:S(2)}) collective-permute-start(f32[3,2,1,4,4,128]{5,4,3,2,1,0:T(4,128)S(1)} %get-tuple-element.239), channel_id=1, source_target_pairs={{1,0},{2,1},{3,2},{4,3},{5,4},{6,5},{7,6},{8,7},{9,8},{10,9},{11,1... | collective-permute-start | bytes 147464 | tf_op jit(solution)/shard_map/ppermute | solution.py:18
  201.0 7.2 %collective-permute-start.14 = (f32[3,2,1,4,4,128]{5,4,3,2,1,0:T(4,128)S(1)}, f32[3,2,1,4,4,128]{5,4,3,2,1,0:T(4,128)S(1)}, u32[]{:S(2)}, u32[]{:S(2)}) collective-permute-start(f32[3,2,1,4,4,128]{5,4,3,2,1,0:T(4,128)S(1)} %get-tuple-element.238), channel_id=1, source_target_pairs={{0,1},{1,2},{2,3},{3,4},{4,5},{5,6},{6,7},{7,8},{8,9},{9,10},{10,1... | collective-permute-start | bytes 147464 | tf_op jit(solution)/shard_map/ppermute | solution.py:17
  209.0 9.5 %collective-permute-start.17 = (f32[3,2,1,4,4,128]{5,4,3,2,1,0:T(4,128)S(1)}, f32[3,2,1,4,4,128]{5,4,3,2,1,0:T(4,128)S(1)}, u32[]{:S(2)}, u32[]{:S(2)}) collective-permute-start(f32[3,2,1,4,4,128]{5,4,3,2,1,0:T(4,128)S(1)} %get-tuple-element.237), channel_id=1, source_target_pairs={{1,0},{2,1},{3,2},{4,3},{5,4},{6,5},{7,6},{8,7},{9,8},{10,9},{11,1... | collective-permute-start | bytes 147464 | tf_op jit(solution)/shard_map/ppermute | solution.py:18
  210.3 8.2 %collective-permute-start.16 = (f32[3,2,1,4,4,128]{5,4,3,2,1,0:T(4,128)S(1)}, f32[3,2,1,4,4,128]{5,4,3,2,1,0:T(4,128)S(1)}, u32[]{:S(2)}, u32[]{:S(2)}) collective-permute-start(f32[3,2,1,4,4,128]{5,4,3,2,1,0:T(4,128)S(1)} %get-tuple-element.236), channel_id=1, source_target_pairs={{0,1},{1,2},{2,3},{3,4},{4,5},{5,6},{6,7},{7,8},{8,9},{9,10},{10,1... | collective-permute-start | bytes 147464 | tf_op jit(solution)/shard_map/ppermute | solution.py:17
  266.8 13.2 %all-to-all-start.4 = ((f32[2,1,4,256]{2,0,1,3:T(2,128)}), f32[2,1,4,256]{2,0,1,3:T(2,128)S(1)}, u32[]{:S(2)}, u32[]{:S(2)}) async-start(f32[2,1,4,256]{2,0,1,3:T(2,128)} %copy.981), calls=%async_computation.4 | async-start | bytes 524288 | tf_op jit(solution)/shard_map/all_to_all | solution.py:159
  270.6 23.3 %collective-permute-start.28 = (f32[2,1,4,12,256]{4,2,3,1,0:T(4,128)S(1)}, f32[2,1,4,12,256]{4,2,3,1,0:T(4,128)S(1)}, u32[]{:S(2)}, u32[]{:S(2)}) collective-permute-start(f32[2,1,4,12,256]{4,2,3,1,0:T(4,128)S(1)} %fusion.1102), channel_id=1, source_target_pairs={{1,0},{2,1},{3,2},{4,3},{5,4},{6,5},{7,6},{8,7},{9,8},{10,9},{11,1... | collective-permute-start | bytes 294920 | tf_op jit(solution)/shard_map/ppermute | solution.py:18
  271.9 22.0 %collective-permute-start.29 = (f32[2,1,4,12,256]{4,2,3,1,0:T(4,128)S(1)}, f32[2,1,4,12,256]{4,2,3,1,0:T(4,128)S(1)}, u32[]{:S(2)}, u32[]{:S(2)}) collective-permute-start(f32[2,1,4,12,256]{4,2,3,1,0:T(4,128)S(1)} %fusion.1102), channel_id=1, source_target_pairs={{0,1},{1,2},{2,3},{3,4},{4,5},{5,6},{6,7},{7,8},{8,9},{9,10},{10,1... | collective-permute-start | bytes 294920 | tf_op jit(solution)/shard_map/ppermute | solution.py:17
  281.5 10.8 %all-to-all-start.6 = ((f32[2,1,128,8]{3,0,1,2:T(2,128)}), f32[2,1,128,8]{3,0,1,2:T(2,128)S(1)}, u32[]{:S(2)}, u32[]{:S(2)}) async-start(f32[2,1,128,8]{3,0,1,2:T(2,128)} %copy.992), calls=%async_computation.6 | async-start | bytes 262144 | tf_op jit(solution)/shard_map/all_to_all | solution.py:131
  284.1 8.4 %collective-permute-start.23 = (f32[3,2,1,4,4,128]{5,4,3,2,1,0:T(4,128)S(1)}, f32[3,2,1,4,4,128]{5,4,3,2,1,0:T(4,128)S(1)}, u32[]{:S(2)}, u32[]{:S(2)}) collective-permute-start(f32[3,2,1,4,4,128]{5,4,3,2,1,0:T(4,128)S(1)} %get-tuple-element.235), channel_id=1, source_target_pairs={{1,0},{2,1},{3,2},{4,3},{5,4},{6,5},{7,6},{8,7},{9,8},{10,9},{11,1... | collective-permute-start | bytes 147464 | tf_op jit(solution)/shard_map/ppermute | solution.py:18
  285.4 7.2 %collective-permute-start.22 = (f32[3,2,1,4,4,128]{5,4,3,2,1,0:T(4,128)S(1)}, f32[3,2,1,4,4,128]{5,4,3,2,1,0:T(4,128)S(1)}, u32[]{:S(2)}, u32[]{:S(2)}) collective-permute-start(f32[3,2,1,4,4,128]{5,4,3,2,1,0:T(4,128)S(1)} %get-tuple-element.234), channel_id=1, source_target_pairs={{0,1},{1,2},{2,3},{3,4},{4,5},{5,6},{6,7},{7,8},{8,9},{9,10},{10,1... | collective-permute-start | bytes 147464 | tf_op jit(solution)/shard_map/ppermute | solution.py:17
  (18 other events, 54.1 us)
